TPU v7x, 32 devices: a whole 2x2x4 slice. The times are simulated.
32 devices in a mesh: req: 16 (over z, x, core), kv: 2 (over y).
Axes of the slice: x: 2, y: 2, z: 4, core: 2. Of those that a mesh axis runs over, the one named last changes fastest.
Arguments:
- hidden: bfloat16 [32, 256, 1024], P('req', 'kv'), may hold values from -6 to 6
- queries: bfloat16 [32, 256, 1024], P('req', 'kv'), may hold values from -24 to 24
- span_kv: bfloat16 [32, 256, 8, 128], P('req', 'kv'), may hold values from -48 to 48
- cache: bfloat16 [32, 2048, 8, 128], P('req', 'kv'), may hold values from -48 to 48
- req_order: int32 [32], replicated, may hold values from 0 to 31, each once
- cached_len: int32 [32], replicated, may hold values from 8 to 2048, as said below
- out_weight: bfloat16 [1024, 1024], replicated, may hold values from -0.1875 to 0.1875
- norm_gain: float32 [1024], replicated, may hold values from 0.1 to 1.9
- expert_ids: int32 [8192, 8], P(('req', 'kv')), may hold values from 0 to 15, all different within a row; in each aligned block of 256 rows (0 to 255, 256 to 511, ...) at most 256 rows name the same one
- expert_weights: float32 [8192, 8], P(('req', 'kv')), may hold values from 0.05 to 0.5
- w_experts: bfloat16 [16, 3, 1024, 512], P('req', None, None, 'kv'), may hold values from -0.25 to 0.25
- block_map: int32 [32, 128], P('req'), may hold values from 0 to 4095, as said below
Outputs:
- layer_out: bfloat16 [32, 256, 1024], P('req', 'kv')
- decode_pool: bfloat16 [4096, 8, 16, 128], P('req', 'kv')
Inputs may be any that keep to these rules, and one draw needn't show every extreme that they name: `cached_len`: some request fills its cache. `block_map`: a permutation of the 4096 pool pages; pool page s belongs to req index s // 256; the pages that one kv index holds of the slots of one req index (positions of its cache share) go to every req index equally often. `expert_ids`: in the rows of one device no expert is named more than 256 times.
All inputs are finite; a program needn't handle non-finite values.
Results may differ from a plain program's by a relative error of at most 0.023.
Values may be sent and summed in bfloat16 or wider, within the bound.
No kernel may reach another device: no remote copies, remote signals or barrier semaphores. Data moves between devices by JAX's collectives and lax.ppermute only.
A program may use at most 128 MiB of HBM per device.

v0:
```python
import math
import jax
import jax.numpy as jnp
from jax import lax
from jax.sharding import PartitionSpec as P

BLOCK = 16


def lookup_lengths(req_order, cached_len, count):
    start = lax.axis_index("req") * count
    mine = lax.dynamic_slice_in_dim(req_order, start, count)
    match = mine[:, None] == jnp.arange(cached_len.shape[0], dtype=jnp.int32)[None, :]
    return jnp.sum(jnp.where(match, cached_len[None, :], 0), axis=1)


def score_block(query_rows, cache_rows, span_rows):
    span_count, group_count, width = query_rows.shape
    head_dim = cache_rows.shape[-1] // 2
    per_group = width // head_dim
    query_split = query_rows.reshape(span_count, group_count, per_group, head_dim)
    key_rows = jnp.concatenate([cache_rows[..., :head_dim], span_rows[..., :head_dim]], axis=0)
    value_rows = jnp.concatenate([cache_rows[..., head_dim:], span_rows[..., head_dim:]], axis=0)
    scores = jnp.einsum(
        "igsd,pgd->gsip", query_split, key_rows, preferred_element_type=jnp.float32
    ) * (1.0 / math.sqrt(head_dim))
    return (scores, value_rows)


def soft_weights(scores, allowed, value_rows):
    masked = jnp.where(allowed, scores, -1e30)
    row_max = jnp.max(masked, axis=-1, keepdims=True)
    probability = jnp.where(allowed, jnp.exp(masked - row_max), 0.0)
    prob_sum = jnp.sum(probability, axis=-1)
    weighted = jnp.einsum(
        "gsip,pgd->igsd",
        probability.astype(jnp.bfloat16),
        value_rows,
        preferred_element_type=jnp.float32,
    )
    return (weighted, jnp.transpose(row_max[..., 0], (2, 0, 1)), jnp.transpose(prob_sum, (2, 0, 1)))


def whole_request(operands):
    query_rows, cache_rows, span_rows, length = operands
    scores, value_rows = score_block(query_rows, cache_rows, span_rows)
    cached = cache_rows.shape[0]
    position = jnp.arange(scores.shape[-1])[None, :]
    query_pos = jnp.arange(query_rows.shape[0])[:, None]
    allowed = jnp.where(position < cached, position < length, position - cached <= query_pos)
    weighted, row_max, prob_sum = soft_weights(scores, allowed, value_rows)
    result = weighted / prob_sum[..., None]
    return result.reshape(query_rows.shape).astype(jnp.bfloat16)


def place_pages(page_rows, slot_numbers, slots_dev):
    owner_index = slot_numbers // slots_dev
    arrangement = jnp.argsort(owner_index, stable=True)
    return (page_rows[arrangement], (slot_numbers % slots_dev)[arrangement])


def body(
    hidden,
    queries,
    span_kv,
    cache,
    req_order,
    cached_len,
    out_weight,
    norm_gain,
    expert_ids,
    expert_weights,
    w_experts,
    block_map,
):
    local_reqs, local_tokens, width_model = hidden.shape
    row_count = local_reqs * local_tokens
    req_count = lax.axis_size("req")
    kv_count = lax.axis_size("kv")
    kv_heads = span_kv.shape[2]
    head_pair = span_kv.shape[3]
    group_width = queries.shape[2] // kv_heads
    group_count = kv_heads // kv_count
    slots_dev = local_reqs * block_map.shape[1]
    lengths = lookup_lengths(req_order, cached_len, local_reqs)
    queries_grouped = queries.reshape(local_reqs, local_tokens, kv_heads, group_width)
    cache_heads, span_heads, query_heads = (
        lax.all_to_all(cache, "kv", split_axis=2, concat_axis=1, tiled=True),
        lax.all_to_all(span_kv, "kv", split_axis=2, concat_axis=1, tiled=True),
        lax.all_to_all(queries_grouped, "kv", split_axis=2, concat_axis=1, tiled=True),
    )
    attn_heads = lax.map(whole_request, (query_heads, cache_heads, span_heads, lengths))
    attn = lax.all_to_all(attn_heads, "kv", split_axis=1, concat_axis=2, tiled=True).reshape(
        row_count, kv_heads * group_width
    )
    page_total = block_map.shape[1]
    visible = jnp.arange(cache_heads.shape[1])[None, :] < lengths[:, None]
    visible_cache = jnp.where(visible[:, :, None, None], cache_heads, jnp.zeros((), jnp.bfloat16))
    page_rows = (
        visible_cache.reshape(local_reqs, page_total, BLOCK, group_count, head_pair)
        .transpose(0, 1, 3, 2, 4)
        .reshape(local_reqs * page_total, group_count, BLOCK, head_pair)
    )
    sorted_pages, local_slot = place_pages(page_rows, block_map.reshape(-1), slots_dev)
    per_owner = sorted_pages.shape[0] // req_count
    outgoing = sorted_pages.reshape(req_count, per_owner, group_count, BLOCK, head_pair)
    arrived, where_to = (
        lax.all_to_all(outgoing, "req", split_axis=0, concat_axis=0, tiled=True),
        lax.all_to_all(
            local_slot.reshape(req_count, per_owner), "req", split_axis=0, concat_axis=0, tiled=True
        ),
    )
    decode_pool = (
        jnp.zeros((slots_dev, group_count, BLOCK, head_pair), jnp.bfloat16)
        .at[where_to.reshape(-1)]
        .set(arrived.reshape(-1, group_count, BLOCK, head_pair))
    )
    residual = hidden.reshape(row_count, width_model).astype(jnp.float32) + jnp.dot(
        attn, out_weight, preferred_element_type=jnp.float32
    )
    inverse_rms = lax.rsqrt(jnp.mean(residual * residual, axis=-1, keepdims=True) + 1e-05)
    normed = (residual * inverse_rms * norm_gain).astype(jnp.bfloat16)
    top_count = expert_ids.shape[1]
    exp_dev = w_experts.shape[0]
    experts = exp_dev * req_count
    capacity = min(row_count, 2 * row_count * top_count // experts)
    chosen = expert_ids.reshape(-1)
    onehot = (chosen[:, None] == jnp.arange(experts, dtype=jnp.int32)[None, :]).astype(jnp.int32)
    slot_rank = jnp.sum(onehot * (jnp.cumsum(onehot, axis=0) - 1), axis=1)
    target = chosen * capacity + slot_rank
    source_row = jnp.arange(chosen.shape[0]) // top_count
    buffer = (
        jnp.zeros((experts * capacity, width_model), jnp.bfloat16)
        .at[target]
        .set(normed[source_row])
        .reshape(experts, capacity, width_model)
    )
    full_weights = lax.all_gather(w_experts, "kv", axis=3, tiled=True)
    slot_block = lax.all_to_all(buffer, "req", split_axis=0, concat_axis=0, tiled=True)
    source_count = slot_block.shape[0] // exp_dev
    grouped = slot_block.reshape(source_count, exp_dev, slot_block.shape[1], width_model)
    gate_act = jnp.einsum(
        "sejd,edf->sejf", grouped, full_weights[:, 0], preferred_element_type=jnp.float32
    )
    up_act = jnp.einsum(
        "sejd,edf->sejf", grouped, full_weights[:, 1], preferred_element_type=jnp.float32
    )
    activated = (jax.nn.silu(gate_act) * up_act).astype(jnp.bfloat16)
    expert_out = jnp.einsum(
        "sejf,edf->sejd", activated, full_weights[:, 2], preferred_element_type=jnp.float32
    ).astype(jnp.bfloat16)
    returned = lax.all_to_all(
        expert_out.reshape(slot_block.shape), "req", split_axis=0, concat_axis=0, tiled=True
    )
    picked = returned.reshape(experts * capacity, width_model)[target].reshape(
        row_count, top_count, width_model
    )
    expert_sum = jnp.sum(expert_weights[..., None] * picked.astype(jnp.float32), axis=1)
    layer_out = (
        (residual + expert_sum).astype(jnp.bfloat16).reshape(local_reqs, local_tokens, width_model)
    )
    return (layer_out, decode_pool)


def solution(mesh):
    return jax.shard_map(
        body,
        mesh=mesh,
        in_specs=(
            P("req", "kv", None),
            P("req", "kv", None),
            P("req", "kv", None, None),
            P("req", "kv", None, None),
            P(),
            P(),
            P(),
            P(),
            P(("req", "kv"), None),
            P(("req", "kv"), None),
            P("req", None, None, "kv"),
            P("req", None),
        ),
        out_specs=(P("req", "kv", None), P("req", "kv", None, None)),
        check_vma=False,
    )
```

profile of v0, /device:TPU:11, one launch (start us, length us, event | category | flops | bytes accessed | tf_op | source)
XLA Modules:
  0.0 748.4 jit_solution(12969157909613193286)
XLA Ops:
  14.9 5.2 all-to-all-done.1
  24.0 5.0 copy.78
  30.1 5.6 all-to-all-start
  52.0 28.7 %all-to-all-done = bf16[2,1024,8,128]{3,1,0,2:T(8,128)(2,1)} async-done(((bf16[2,1024,8,128]{3,1,0,2:T(8,128)(2,1)}), bf16[2,1024,8,128]{3,1,0,2:T(8,128)(2,1)}, u32[]{:S(2)}, u32[]{:S(2)}) %all-to-all-start) | async-done | bytes 4194336 | tf_op jit(solution)/shard_map/all_to_all | solution.py:88
  85.3 104.1 %while.12 = (s32[]{:T(128)}, bf16[2,256,4,128]{3,2,0,1:T(4,128)(2,1)}, bf16[2,2048,4,128]{3,1,2,0:T(8,128)(2,1)}, bf16[2,256,4,128]{1,3,2,0:T(8,128)(2,1)}, s32[...) while((s32[]{:T(128)}, bf16[2,256,4,128]{3,2,0,1:T(4,128)(2,1)}, ...), condition=%wide.region_4.5_spmd, body=%wide.region_1.4_spmd.sunk | while | flops 1251877888 | bytes 80653984 | solution.py:92
  97.6 9.2 %fusion.65 = f32[4,2304,256,2]{2,1,3,0:T(8,128)} fusion(bf16[256,4,2,64]{0,3,2,1:T(8,128)(2,1)S(1)} %bitcast.190, bf16[256,4,64]{0,2,1:T(8,128)(2,1)} %get-tuple-element.183, bf16[2048,4,64]{0,2,1:T(8,128)(2,1)} %get-tuple-element.184), kind=kOutput, calls=%fused_computation.24.clone.1 | convolution fusion | flops 606339072 | bytes 20316160 | tf_op jit(solution)/shard_map/while/body/eval_jaxpr/igsd,pgd->gsip/dot_general | solution.py:24
  111.4 19.4 %fusion.67 = (f32[4,2,256]{2,1,0:T(2,128)S(1)}, bf16[4,2,256,2304]{2,3,1,0:T(8,128)(2,1)}) fusion(f32[4,2304,256,2]{2,1,3,0:T(8,128)} %fusion.65, pred[256,2304]{0,1:T(8,128)(4,1)} %fusion.66), kind=kOutput, calls=%fused_computation.99.clone.1 | output fusion | flops 37751040 | bytes 28909568 | tf_op jit(solution)/shard_map/while/body/eval_jaxpr/sub | solution.py:33
  130.9 5.5 fusion.68
  149.7 9.2 %fusion.65 = f32[4,2304,256,2]{2,1,3,0:T(8,128)} fusion(bf16[256,4,2,64]{0,3,2,1:T(8,128)(2,1)S(1)} %bitcast.190, bf16[256,4,64]{0,2,1:T(8,128)(2,1)} %get-tuple-element.183, bf16[2048,4,64]{0,2,1:T(8,128)(2,1)} %get-tuple-element.184), kind=kOutput, calls=%fused_computation.24.clone.1 | convolution fusion | flops 606339072 | bytes 20316160 | tf_op jit(solution)/shard_map/while/body/eval_jaxpr/igsd,pgd->gsip/dot_general | solution.py:24
  163.5 19.4 %fusion.67 = (f32[4,2,256]{2,1,0:T(2,128)S(1)}, bf16[4,2,256,2304]{2,3,1,0:T(8,128)(2,1)}) fusion(f32[4,2304,256,2]{2,1,3,0:T(8,128)} %fusion.65, pred[256,2304]{0,1:T(8,128)(4,1)} %fusion.66), kind=kOutput, calls=%fused_computation.99.clone.1 | output fusion | flops 37751040 | bytes 28909568 | tf_op jit(solution)/shard_map/while/body/eval_jaxpr/sub | solution.py:33
  182.9 5.5 fusion.68
  198.4 10.7 %all-to-all-start.6 = ((s32[16,1,16]{2,1,0:T(1,128)}), s32[16,1,16]{2,1,0:T(1,128)S(1)}, u32[]{:S(2)}, u32[]{:S(2)}) async-start(s32[16,1,16]{2,1,0:T(1,128)} %all_to_all.84), calls=%async_computation.6 | async-start | bytes 16384 | tf_op jit(solution)/shard_map/all_to_all | solution.py:109
  213.5 33.0 %scatter_custom_fusion = bf16[4096,1024]{1,0:T(8,128)(2,1)} fusion(s32[2048]{0:T(1024)S(1)} %bitcast.205, bf16[256,1024]{1,0:T(8,128)(2,1)} %multiply_convert_fusion, s32[2048]{0:T(1024)S(1)} %broadcast_clamp_fusion.1, bf16[]{:T(256)} %constant.114.clone.1), kind=kCustom, calls=%fused_computation.49 | custom fusion | bytes 8389120 | tf_op jit(solution)/shard_map/scatter | solution.py:135
  246.4 6.4 all-to-all-start.4
  259.4 5.2 gather_fusion.2
  264.6 170.4 %all-to-all-done.4 = bf16[16,256,1024]{2,1,0:T(8,128)(2,1)} async-done(((bf16[16,256,1024]{2,1,0:T(8,128)(2,1)}), bf16[16,256,1024]{2,1,0:T(8,128)(2,1)}, u32[]{:S(2)}, u32[]{:S(2)}) %all-to-all-start.4) | async-done | bytes 8388640 | tf_op jit(solution)/shard_map/all_to_all | solution.py:139
  440.6 46.2 %all-gather.2.cloned.1.call-done = bf16[1,3,1024,512]{3,2,1,0:T(8,128)(2,1)} async-done(((bf16[1,3,1024,256]{3,2,1,0:T(8,128)(2,1)}), bf16[1,3,1024,512]{3,2,1,0:T(8,128)(2,1)}) %all-gather.2.cloned.1.call-update) | async-done | bytes 3145744 | tf_op jit(solution)/shard_map/all_gather | solution.py:138
  486.8 11.4 %fusion.38 = f32[16,256,512]{2,1,0:T(8,128)} fusion(bf16[16,256,1024]{2,1,0:T(8,128)(2,1)} %all-to-all-done.4, bf16[1,3,1024,512]{3,2,1,0:T(8,128)(2,1)} %all-gather.2.cloned.1.call-done), kind=kOutput, calls=%fused_computation.58 | convolution fusion | flops 4294967296 | bytes 17825792 | tf_op jit(solution)/shard_map/sejd,edf->sejf/dot_general | solution.py:142
  498.2 16.0 %convolution_convert_fusion = bf16[16,256,1024]{2,1,0:T(8,128)(2,1)} fusion(f32[16,256,512]{2,1,0:T(8,128)} %fusion.38, bf16[16,256,1024]{2,1,0:T(8,128)(2,1)} %all-to-all-done.4, bf16[1,3,1024,512]{3,2,1,0:T(8,128)(2,1)} %all-gather.2.cloned.1.call-done), kind=kOutput, calls=%fused_computation.47 | convolution fusion | flops 8606711808 | bytes 27262976 | tf_op jit(solution)/shard_map/sejf,edf->sejd/dot_general | solution.py:149
  514.2 18.2 %all-to-all-done.7 = bf16[16,16,4,16,128]{4,3,2,1,0:T(8,128)(2,1)} async-done(((bf16[16,16,4,16,128]{4,3,2,1,0:T(8,128)(2,1)}), bf16[16,16,4,16,128]{4,3,2,1,0:T(8,128)(2,1)}, u32[]{:S(2)}, u32[]{:S(2)}) %all-to-all-start.7) | async-done | bytes 4194336 | tf_op jit(solution)/shard_map/all_to_all | solution.py:108
  532.4 5.3 all-to-all-start.5
  542.2 33.5 %scatter_fusion = bf16[256,4,16,128]{3,2,1,0:T(8,128)(2,1)} fusion(bf16[256,4,16,128]{3,2,1,0:T(8,128)(2,1)} %broadcast_in_dim.106, s32[256]{0:T(256)S(1)} %bitcast.209, bf16[256,4,16,128]{3,2,1,0:T(8,128)(2,1)} %bitcast.57), kind=kCustom, calls=%fused_computation.5 | custom fusion | bytes 12583936 | tf_op jit(solution)/shard_map/scatter | solution.py:116
  575.7 144.2 %all-to-all-done.5 = bf16[16,256,1024]{2,1,0:T(8,128)(2,1)} async-done(((bf16[16,256,1024]{2,1,0:T(8,128)(2,1)}), bf16[16,256,1024]{2,1,0:T(8,128)(2,1)}, u32[]{:S(2)}, u32[]{:S(2)}) %all-to-all-start.5) | async-done | bytes 8388640 | tf_op jit(solution)/shard_map/all_to_all | solution.py:152
  719.9 15.5 %gather_fusion = bf16[2048,1024]{1,0:T(8,128)(2,1)} fusion(bf16[4096,1024]{1,0:T(8,128)(2,1)} %bitcast.46, s32[2048]{0:T(1024)S(1)} %broadcast_clamp_fusion), kind=kCustom, calls=%fused_computation.1 | custom fusion | bytes 8396800 | tf_op jit(solution)/shard_map/gather | solution.py:155
  (113 shorter events, 104.9 us)
Async XLA Ops:
  7.2 203.3 %copy-start = (bf16[1024,1024]{1,0:T(8,128)(2,1)S(1)}, bf16[1024,1024]{1,0:T(8,128)(2,1)}, u32[]{:S(2)}) copy-start(bf16[1024,1024]{1,0:T(8,128)(2,1)} %param.20) | copy-start | bytes 6291460
  7.2 16.5 %copy-start.4 = (s32[256,8]{0,1:T(8,128)S(1)}, s32[256,8]{0,1:T(8,128)}, u32[]{:S(2)}) copy-start(s32[256,8]{0,1:T(8,128)} %param.22) | copy-start | bytes 24580
  9.3 10.9 %all-to-all-start.1 = ((bf16[2,128,8,128]{3,1,0,2:T(8,128)(2,1)}), bf16[2,128,8,128]{3,1,0,2:T(8,128)(2,1)S(1)}, u32[]{:S(2)}, u32[]{:S(2)}) async-start(bf16[2,128,8,128]{3,1,0,2:T(8,128)(2,1)} %copy.81), calls=%async_computation.1 | async-start | bytes 1048576 | tf_op jit(solution)/shard_map/all_to_all | solution.py:89
  20.1 9.9 %all-to-all-start.2 = ((bf16[2,128,8,128]{1,3,0,2:T(8,128)(2,1)}), bf16[2,128,8,128]{1,3,0,2:T(8,128)(2,1)S(1)}, u32[]{:S(2)}, u32[]{:S(2)}) async-start(bf16[2,128,8,128]{1,3,0,2:T(8,128)(2,1)} %copy.84), calls=%async_computation.2 | async-start | bytes 1048576 | tf_op jit(solution)/shard_map/all_to_all | solution.py:90
  29.0 12.1 %copy-start.10 = (s32[32]{0:T(128)S(1)}, s32[32]{0:T(128)}, u32[]{:S(2)}) copy-start(s32[32]{0:T(128)} %param.18) | copy-start | bytes 388
  29.0 12.2 %copy-start.9 = (s32[2,128]{1,0:T(2,128)S(1)}, s32[2,128]{1,0:T(2,128)}, u32[]{:S(2)}) copy-start(s32[2,128]{1,0:T(2,128)} %param.25) | copy-start | bytes 3076
  29.0 16.0 %copy-start.11 = (s32[32]{0:T(128)S(1)}, s32[32]{0:T(128)}, u32[]{:S(2)}) copy-start(s32[32]{0:T(128)} %param.19) | copy-start | bytes 388
  30.1 50.6 %all-to-all-start = ((bf16[2,1024,8,128]{3,1,0,2:T(8,128)(2,1)}), bf16[2,1024,8,128]{3,1,0,2:T(8,128)(2,1)}, u32[]{:S(2)}, u32[]{:S(2)}) async-start(bf16[2,1024,8,128]{3,1,0,2:T(8,128)(2,1)} %copy.78), calls=%async_computation | async-start | bytes 8388608 | tf_op jit(solution)/shard_map/all_to_all | solution.py:88
  85.3 107.8 %copy-start.8 = (s32[256]{0:T(256)S(1)}, s32[256]{0:T(256)}, u32[]{:S(2)}) copy-start(s32[256]{0:T(256)} %compare_select_fusion.3) | copy-start | bytes 3076
  85.3 107.8 %copy-start.1 = (s32[256]{0:T(256)S(1)}, s32[256]{0:T(256)}, u32[]{:S(2)}) copy-start(s32[256]{0:T(256)} %get-tuple-element.133) | copy-start | bytes 3076
  92.3 2.8 copy-start.2
  92.3 3.5 copy-start.3
  144.4 2.8 copy-start.2
  144.4 3.5 copy-start.3
  189.4 23.1 %copy-start.7 = (f32[1024]{0:T(1024)S(1)}, f32[1024]{0:T(1024)}, u32[]{:S(2)}) copy-start(f32[1024]{0:T(1024)} %param.21) | copy-start | bytes 12292
  189.4 9.0 %all-to-all-start.3 = ((bf16[2,256,4,128]{3,2,0,1:T(4,128)(2,1)}), bf16[2,256,4,128]{3,2,0,1:T(4,128)(2,1)S(1)}, u32[]{:S(2)}, u32[]{:S(2)}) async-start(bf16[2,256,4,128]{3,2,0,1:T(4,128)(2,1)} %get-tuple-element.80), calls=%async_computation.3 | async-start | bytes 1048576 | tf_op jit(solution)/shard_map/all_to_all | solution.py:93
  195.0 18.4 %copy-start.5 = (s32[2048,1]{0,1:T(1,128)S(1)}, s32[2048,1]{0,1:T(1,128)}, u32[]{:S(2)}) copy-start(s32[2048,1]{0,1:T(1,128)} %compare_select_fusion.1) | copy-start | bytes 24580
  198.4 48.0 %all-to-all-start.6 = ((s32[16,1,16]{2,1,0:T(1,128)}), s32[16,1,16]{2,1,0:T(1,128)S(1)}, u32[]{:S(2)}, u32[]{:S(2)}) async-start(s32[16,1,16]{2,1,0:T(1,128)} %all_to_all.84), calls=%async_computation.6 | async-start | bytes 16384 | tf_op jit(solution)/shard_map/all_to_all | solution.py:109
  246.4 188.6 %all-to-all-start.4 = ((bf16[16,256,1024]{2,1,0:T(8,128)(2,1)}), bf16[16,256,1024]{2,1,0:T(8,128)(2,1)}, u32[]{:S(2)}, u32[]{:S(2)}) async-start(bf16[16,256,1024]{2,1,0:T(8,128)(2,1)} %bitcast.189), calls=%async_computation.4 | async-start | bytes 16777216 | tf_op jit(solution)/shard_map/all_to_all | solution.py:139
  435.0 97.4 %all-to-all-start.7 = ((bf16[16,16,4,16,128]{4,3,2,1,0:T(8,128)(2,1)}), bf16[16,16,4,16,128]{4,3,2,1,0:T(8,128)(2,1)}, u32[]{:S(2)}, u32[]{:S(2)}) async-start(bf16[16,16,4,16,128]{4,3,2,1,0:T(8,128)(2,1)} %bitcast.192), calls=%async_computation.7 | async-start | bytes 8388608 | tf_op jit(solution)/shard_map/all_to_all | solution.py:108
  439.9 46.9 %all-gather.2.cloned.1.call-start = ((), (), s32[]{:S(2)}) async-start(), calls=%async_computation.8 | async-start | bytes 4718592 | tf_op jit(solution)/shard_map/all_gather | solution.py:138
  514.2 23.5 %copy-start.6 = (f32[256,8]{0,1:T(8,128)S(1)}, f32[256,8]{0,1:T(8,128)}, u32[]{:S(2)}) copy-start(f32[256,8]{0,1:T(8,128)} %param.23) | copy-start | bytes 24580
  532.4 187.5 %all-to-all-start.5 = ((bf16[16,256,1024]{2,1,0:T(8,128)(2,1)}), bf16[16,256,1024]{2,1,0:T(8,128)(2,1)}, u32[]{:S(2)}, u32[]{:S(2)}) async-start(bf16[16,256,1024]{2,1,0:T(8,128)(2,1)} %convolution_convert_fusion), calls=%async_computation.5 | async-start | bytes 16777216 | tf_op jit(solution)/shard_map/all_to_all | solution.py:152
Sparse Core Ops, SparseCore 0:
  442.3 44.5 all-gather.1
where the time goes:
time: 760 us; the launch traced here: 748 us
  waiting for transfers between devices  417 us (55%)
  local copies, waits for them, and re-layouts  147 us (19%)
  other arithmetic  68.1 us (9%)
  matrix products  58.8 us (8%)
  starting transfers between devices  43.5 us (6%)
  between operations  14.8 us (2%)
    all_to_all x1, waiting for transfers between devices, body(): lax.all_to_all(buffer, 'req', split_axis=0, concat_axis=0, tiled=True)  170 us
    all_to_all x1, waiting for transfers between devices, body(): lax.all_to_all(expert_out.reshape(slot_block.shape), 'req', split_axis=0,...  144 us
    all_gather x1, waiting for transfers between devices, body(): full_weights = lax.all_gather(w_experts, 'kv', axis=3, tiled=True)  46.2 us
    sub x2, other arithmetic, soft_weights(): probability = jnp.where(allowed, jnp.exp(masked - row_max), 0.0)  38.9 us
    scatter x1, local copies, waits for them, and re-layouts, body(): decode_pool = jnp.zeros((slots_dev, group_count, BLOCK, head_pair), jnp.b...  33.5 us
    scatter x1, local copies, waits for them, and re-layouts, body(): buffer = jnp.zeros((experts * capacity, width_model), jnp.bfloat16).at[ta...  33 us
    all_to_all x1, waiting for transfers between devices, body(): lax.all_to_all(cache, 'kv', split_axis=2, concat_axis=1, tiled=True)  28.7 us
    dynamic_slice x10, local copies, waits for them, and re-layouts, body(): lax.map(whole_request, (query_heads, cache_heads, span_heads, lengths))  20.2 us
  transfers between devices with their start and end apart: 9, of which 8 were waited for; matrix products, arithmetic and copies ran while one was open for 19% of the time, Pallas kernels for 0%

commit v1 on v0

--- a/solution.py
+++ b/solution.py
@@ -135,7 +135,15 @@
         .set(normed[source_row])
         .reshape(experts, capacity, width_model)
     )
-    full_weights = lax.all_gather(w_experts, "kv", axis=3, tiled=True)
+    ways, here = (lax.axis_size("kv"), lax.axis_index("kv"))
+    grown, reach = (w_experts, 1)
+    while reach < ways:
+        theirs = lax.ppermute(grown, "kv", [(d, d ^ reach) for d in range(ways)])
+        mine_first = jnp.concatenate([grown, theirs], axis=3)
+        theirs_first = jnp.concatenate([theirs, grown], axis=3)
+        grown = jnp.where(here & reach == 0, mine_first, theirs_first)
+        reach = 2 * reach
+    full_weights = grown
     slot_block = lax.all_to_all(buffer, "req", split_axis=0, concat_axis=0, tiled=True)
     source_count = slot_block.shape[0] // exp_dev
     grouped = slot_block.reshape(source_count, exp_dev, slot_block.shape[1], width_model)

time: 760 us -> 760 us (level)
  local copies, waits for them, and re-layouts: 147 us -> 164 us
  between operations: 14.8 us -> 1.18 us
    all_gather x1 -> x0, waiting for transfers between devices: 46.2 us -> none  [body(): full_weights = lax.all_gather(w_experts, 'kv', axis=3, tiled=True)]
    ppermute x0 -> x1, waiting for transfers between devices: none -> 35.9 us  [body(): theirs = lax.ppermute(grown, 'kv', [(d, d ^ reach) for d in range(ways)])]
    all_to_all x0 -> x1, local copies, waits for them, and re-layouts: none -> 12.3 us  [body(): lax.all_to_all(expert_out.reshape(slot_block.shape), 'req', split_axis=0,...]
where the time goes in v1:
time: 760 us; the launch traced here: 748 us
  waiting for transfers between devices  410 us (54%)
  local copies, waits for them, and re-layouts  164 us (22%)
  other arithmetic  71.7 us (9%)
  matrix products  57 us (8%)
  starting transfers between devices  43.7 us (6%)
    all_to_all x1, waiting for transfers between devices, body(): lax.all_to_all(buffer, 'req', split_axis=0, concat_axis=0, tiled=True)  170 us
    all_to_all x1, waiting for transfers between devices, body(): lax.all_to_all(expert_out.reshape(slot_block.shape), 'req', split_axis=0,...  144 us
    sub x2, other arithmetic, soft_weights(): probability = jnp.where(allowed, jnp.exp(masked - row_max), 0.0)  38.9 us
    ppermute x1, waiting for transfers between devices, body(): theirs = lax.ppermute(grown, 'kv', [(d, d ^ reach) for d in range(ways)])  35.9 us
    scatter x1, local copies, waits for them, and re-layouts, body(): buffer = jnp.zeros((experts * capacity, width_model), jnp.bfloat16).at[ta...  33.9 us
    scatter x1, local copies, waits for them, and re-layouts, body(): decode_pool = jnp.zeros((slots_dev, group_count, BLOCK, head_pair), jnp.b...  33.5 us
    all_to_all x1, waiting for transfers between devices, body(): lax.all_to_all(cache, 'kv', split_axis=2, concat_axis=1, tiled=True)  28.7 us
    all_to_all x1, waiting for transfers between devices, body(): lax.all_to_all(outgoing, 'req', split_axis=0, concat_axis=0, tiled=True)  23 us
  transfers between devices with their start and end apart: 9, of which 8 were waited for; matrix products, arithmetic and copies ran while one was open for 19% of the time, Pallas kernels for 0%

profile of v1, /device:TPU:11, one launch (start us, length us, event | category | flops | bytes accessed | tf_op | source)
XLA Modules:
  0.0 748.2 jit_solution(6504406986900866038)
XLA Ops:
  8.4 5.2 all-to-all-done.1
  23.6 5.6 all-to-all-start
  45.5 28.7 %all-to-all-done = bf16[2,1024,8,128]{3,1,0,2:T(8,128)(2,1)} async-done(((bf16[2,1024,8,128]{3,1,0,2:T(8,128)(2,1)}), bf16[2,1024,8,128]{3,1,0,2:T(8,128)(2,1)}, u32[]{:S(2)}, u32[]{:S(2)}) %all-to-all-start) | async-done | bytes 4194336 | tf_op jit(solution)/shard_map/all_to_all | solution.py:88
  78.7 104.1 %while.12 = (s32[]{:T(128)}, bf16[2,256,4,128]{3,2,0,1:T(4,128)(2,1)}, bf16[2,2048,4,128]{3,1,2,0:T(8,128)(2,1)}, bf16[2,256,4,128]{1,3,2,0:T(8,128)(2,1)}, s32[...) while((s32[]{:T(128)}, bf16[2,256,4,128]{3,2,0,1:T(4,128)(2,1)}, ...), condition=%wide.region_4.5_spmd, body=%wide.region_1.4_spmd.sunk | while | flops 1251877888 | bytes 80653984 | solution.py:92
  91.1 9.2 %fusion.65 = f32[4,2304,256,2]{2,1,3,0:T(8,128)} fusion(bf16[256,4,2,64]{0,3,2,1:T(8,128)(2,1)S(1)} %bitcast.193, bf16[256,4,64]{0,2,1:T(8,128)(2,1)} %get-tuple-element.183, bf16[2048,4,64]{0,2,1:T(8,128)(2,1)} %get-tuple-element.184), kind=kOutput, calls=%fused_computation.24.clone.1 | convolution fusion | flops 606339072 | bytes 20316160 | tf_op jit(solution)/shard_map/while/body/eval_jaxpr/igsd,pgd->gsip/dot_general | solution.py:24
  104.9 19.4 %fusion.67 = (f32[4,2,256]{2,1,0:T(2,128)S(1)}, bf16[4,2,256,2304]{2,3,1,0:T(8,128)(2,1)}) fusion(f32[4,2304,256,2]{2,1,3,0:T(8,128)} %fusion.65, pred[256,2304]{0,1:T(8,128)(4,1)} %fusion.66), kind=kOutput, calls=%fused_computation.100.clone.1 | output fusion | flops 37751040 | bytes 28909568 | tf_op jit(solution)/shard_map/while/body/eval_jaxpr/sub | solution.py:33
  124.3 5.5 fusion.68
  143.2 9.2 %fusion.65 = f32[4,2304,256,2]{2,1,3,0:T(8,128)} fusion(bf16[256,4,2,64]{0,3,2,1:T(8,128)(2,1)S(1)} %bitcast.193, bf16[256,4,64]{0,2,1:T(8,128)(2,1)} %get-tuple-element.183, bf16[2048,4,64]{0,2,1:T(8,128)(2,1)} %get-tuple-element.184), kind=kOutput, calls=%fused_computation.24.clone.1 | convolution fusion | flops 606339072 | bytes 20316160 | tf_op jit(solution)/shard_map/while/body/eval_jaxpr/igsd,pgd->gsip/dot_general | solution.py:24
  157.0 19.4 %fusion.67 = (f32[4,2,256]{2,1,0:T(2,128)S(1)}, bf16[4,2,256,2304]{2,3,1,0:T(8,128)(2,1)}) fusion(f32[4,2304,256,2]{2,1,3,0:T(8,128)} %fusion.65, pred[256,2304]{0,1:T(8,128)(4,1)} %fusion.66), kind=kOutput, calls=%fused_computation.100.clone.1 | output fusion | flops 37751040 | bytes 28909568 | tf_op jit(solution)/shard_map/while/body/eval_jaxpr/sub | solution.py:33
  176.4 5.5 fusion.68
  191.9 11.0 %all-to-all-start.6 = ((s32[16,1,16]{2,1,0:T(1,128)}), s32[16,1,16]{2,1,0:T(1,128)S(1)}, u32[]{:S(2)}, u32[]{:S(2)}) async-start(s32[16,1,16]{2,1,0:T(1,128)} %all_to_all.84), calls=%async_computation.6 | async-start | bytes 16384 | tf_op jit(solution)/shard_map/all_to_all | solution.py:109
  207.2 33.9 %scatter_custom_fusion = bf16[4096,1024]{1,0:T(8,128)(2,1)} fusion(s32[2048]{0:T(1024)S(1)} %bitcast.208, bf16[256,1024]{1,0:T(8,128)(2,1)} %multiply_convert_fusion, s32[2048]{0:T(1024)S(1)} %broadcast_clamp_fusion.1, bf16[]{:T(256)} %constant.117.clone.1), kind=kCustom, calls=%fused_computation.49 | custom fusion | bytes 8389120 | tf_op jit(solution)/shard_map/scatter | solution.py:135
  241.1 6.3 all-to-all-start.4
  254.1 5.2 gather_fusion.2
  259.3 170.4 %all-to-all-done.4 = bf16[16,256,1024]{2,1,0:T(8,128)(2,1)} async-done(((bf16[16,256,1024]{2,1,0:T(8,128)(2,1)}), bf16[16,256,1024]{2,1,0:T(8,128)(2,1)}, u32[]{:S(2)}, u32[]{:S(2)}) %all-to-all-start.4) | async-done | bytes 8388640 | tf_op jit(solution)/shard_map/all_to_all | solution.py:147
  437.1 35.9 %collective-permute-done = bf16[1,3,1024,256]{2,3,1,0:T(8,128)(2,1)} collective-permute-done((bf16[1,3,1024,256]{2,3,1,0:T(8,128)(2,1)}, bf16[1,3,1024,256]{2,3,1,0:T(8,128)(2,1)}, u32[]{:S(2)}, u32[]{:S(2)}) %collective-permute-start) | collective-permute-done | bytes 1572896 | tf_op jit(solution)/shard_map/ppermute | solution.py:141
  478.4 10.1 %fusion.38 = f32[512,16,256]{2,0,1:T(8,128)} fusion(bf16[16,256,1024]{2,1,0:T(8,128)(2,1)} %all-to-all-done.4, bf16[1,3,1024,512]{2,3,1,0:T(8,128)(2,1)S(1)} %maximum_select_fusion), kind=kOutput, calls=%fused_computation.58 | convolution fusion | flops 4294967296 | bytes 17825792 | tf_op jit(solution)/shard_map/sejd,edf->sejf/dot_general | solution.py:150
  488.5 15.5 %convert_bitcast_fusion = bf16[16,256,1024]{1,2,0:T(8,128)(2,1)} fusion(f32[512,16,256]{2,0,1:T(8,128)} %fusion.38, bf16[16,256,1024]{2,1,0:T(8,128)(2,1)} %all-to-all-done.4, bf16[1,3,1024,512]{2,3,1,0:T(8,128)(2,1)} %copy-done.4), kind=kOutput, calls=%fused_computation.47 | convolution fusion | flops 8606711808 | bytes 27262976 | tf_op jit(solution)/shard_map/sejf,edf->sejd/dot_general | solution.py:157
  504.0 23.0 %all-to-all-done.7 = bf16[16,16,4,16,128]{4,3,2,1,0:T(8,128)(2,1)} async-done(((bf16[16,16,4,16,128]{4,3,2,1,0:T(8,128)(2,1)}), bf16[16,16,4,16,128]{4,3,2,1,0:T(8,128)(2,1)}, u32[]{:S(2)}, u32[]{:S(2)}) %all-to-all-start.7) | async-done | bytes 4194336 | tf_op jit(solution)/shard_map/all_to_all | solution.py:108
  527.0 5.3 all-to-all-start.5
  536.8 33.5 %scatter_fusion = bf16[256,4,16,128]{3,2,1,0:T(8,128)(2,1)} fusion(bf16[256,4,16,128]{3,2,1,0:T(8,128)(2,1)} %broadcast_in_dim.106, s32[256]{0:T(256)S(1)} %bitcast.212, bf16[256,4,16,128]{3,2,1,0:T(8,128)(2,1)} %bitcast.57), kind=kCustom, calls=%fused_computation.5 | custom fusion | bytes 12583936 | tf_op jit(solution)/shard_map/scatter | solution.py:116
  570.3 144.2 %all-to-all-done.5 = bf16[16,256,1024]{1,2,0:T(8,128)(2,1)} async-done(((bf16[16,256,1024]{1,2,0:T(8,128)(2,1)}), bf16[16,256,1024]{1,2,0:T(8,128)(2,1)}, u32[]{:S(2)}, u32[]{:S(2)}) %all-to-all-start.5) | async-done | bytes 8388640 | tf_op jit(solution)/shard_map/all_to_all | solution.py:160
  714.5 12.3 %copy.129 = bf16[16,256,1024]{2,1,0:T(8,128)(2,1)} copy(bf16[16,256,1024]{1,2,0:T(8,128)(2,1)} %all-to-all-done.5) | data formatting | bytes 16777216 | tf_op jit(solution)/shard_map/all_to_all | solution.py:160
  726.8 15.4 %gather_fusion = bf16[2048,1024]{1,0:T(8,128)(2,1)} fusion(bf16[4096,1024]{1,0:T(8,128)(2,1)} %bitcast.188, s32[2048]{0:T(1024)S(1)} %broadcast_clamp_fusion), kind=kCustom, calls=%fused_computation.1 | custom fusion | bytes 8396800 | tf_op jit(solution)/shard_map/gather | solution.py:163
  (117 shorter events, 117.1 us)
Async XLA Ops:
  0.6 203.6 %copy-start = (bf16[1024,1024]{1,0:T(8,128)(2,1)S(1)}, bf16[1024,1024]{1,0:T(8,128)(2,1)}, u32[]{:S(2)}) copy-start(bf16[1024,1024]{1,0:T(8,128)(2,1)} %param.20) | copy-start | bytes 6291460
  0.6 16.5 %copy-start.5 = (s32[256,8]{0,1:T(8,128)S(1)}, s32[256,8]{0,1:T(8,128)}, u32[]{:S(2)}) copy-start(s32[256,8]{0,1:T(8,128)} %param.22) | copy-start | bytes 24580
  2.7 10.9 %all-to-all-start.1 = ((bf16[2,128,8,128]{3,1,0,2:T(8,128)(2,1)}), bf16[2,128,8,128]{3,1,0,2:T(8,128)(2,1)S(1)}, u32[]{:S(2)}, u32[]{:S(2)}) async-start(bf16[2,128,8,128]{3,1,0,2:T(8,128)(2,1)} %copy.110), calls=%async_computation.1 | async-start | bytes 1048576 | tf_op jit(solution)/shard_map/all_to_all | solution.py:89
  13.6 9.9 %all-to-all-start.2 = ((bf16[2,128,8,128]{1,3,0,2:T(8,128)(2,1)}), bf16[2,128,8,128]{1,3,0,2:T(8,128)(2,1)S(1)}, u32[]{:S(2)}, u32[]{:S(2)}) async-start(bf16[2,128,8,128]{1,3,0,2:T(8,128)(2,1)} %copy.113), calls=%async_computation.2 | async-start | bytes 1048576 | tf_op jit(solution)/shard_map/all_to_all | solution.py:90
  22.5 12.1 %copy-start.11 = (s32[32]{0:T(128)S(1)}, s32[32]{0:T(128)}, u32[]{:S(2)}) copy-start(s32[32]{0:T(128)} %param.18) | copy-start | bytes 388
  22.5 12.2 %copy-start.10 = (s32[2,128]{1,0:T(2,128)S(1)}, s32[2,128]{1,0:T(2,128)}, u32[]{:S(2)}) copy-start(s32[2,128]{1,0:T(2,128)} %param.25) | copy-start | bytes 3076
  22.5 16.0 %copy-start.12 = (s32[32]{0:T(128)S(1)}, s32[32]{0:T(128)}, u32[]{:S(2)}) copy-start(s32[32]{0:T(128)} %param.19) | copy-start | bytes 388
  23.6 50.6 %all-to-all-start = ((bf16[2,1024,8,128]{3,1,0,2:T(8,128)(2,1)}), bf16[2,1024,8,128]{3,1,0,2:T(8,128)(2,1)}, u32[]{:S(2)}, u32[]{:S(2)}) async-start(bf16[2,1024,8,128]{3,1,0,2:T(8,128)(2,1)} %copy.107), calls=%async_computation | async-start | bytes 8388608 | tf_op jit(solution)/shard_map/all_to_all | solution.py:88
  78.7 107.8 %copy-start.9 = (s32[256]{0:T(256)S(1)}, s32[256]{0:T(256)}, u32[]{:S(2)}) copy-start(s32[256]{0:T(256)} %compare_select_fusion.3) | copy-start | bytes 3076
  78.7 107.8 %copy-start.1 = (s32[256]{0:T(256)S(1)}, s32[256]{0:T(256)}, u32[]{:S(2)}) copy-start(s32[256]{0:T(256)} %get-tuple-element.133) | copy-start | bytes 3076
  85.8 2.8 copy-start.2
  85.8 3.5 copy-start.3
  137.8 2.8 copy-start.2
  137.8 3.5 copy-start.3
  182.9 23.4 %copy-start.8 = (f32[1024]{0:T(1024)S(1)}, f32[1024]{0:T(1024)}, u32[]{:S(2)}) copy-start(f32[1024]{0:T(1024)} %param.21) | copy-start | bytes 12292
  182.9 9.0 %all-to-all-start.3 = ((bf16[2,256,4,128]{3,2,0,1:T(4,128)(2,1)}), bf16[2,256,4,128]{3,2,0,1:T(4,128)(2,1)S(1)}, u32[]{:S(2)}, u32[]{:S(2)}) async-start(bf16[2,256,4,128]{3,2,0,1:T(4,128)(2,1)} %get-tuple-element.80), calls=%async_computation.3 | async-start | bytes 1048576 | tf_op jit(solution)/shard_map/all_to_all | solution.py:93
  188.5 18.7 %copy-start.6 = (s32[2048,1]{0,1:T(1,128)S(1)}, s32[2048,1]{0,1:T(1,128)}, u32[]{:S(2)}) copy-start(s32[2048,1]{0,1:T(1,128)} %compare_select_fusion.1) | copy-start | bytes 24580
  191.9 49.2 %all-to-all-start.6 = ((s32[16,1,16]{2,1,0:T(1,128)}), s32[16,1,16]{2,1,0:T(1,128)S(1)}, u32[]{:S(2)}, u32[]{:S(2)}) async-start(s32[16,1,16]{2,1,0:T(1,128)} %all_to_all.84), calls=%async_computation.6 | async-start | bytes 16384 | tf_op jit(solution)/shard_map/all_to_all | solution.py:109
  241.1 188.5 %all-to-all-start.4 = ((bf16[16,256,1024]{2,1,0:T(8,128)(2,1)}), bf16[16,256,1024]{2,1,0:T(8,128)(2,1)}, u32[]{:S(2)}, u32[]{:S(2)}) async-start(bf16[16,256,1024]{2,1,0:T(8,128)(2,1)} %bitcast.192), calls=%async_computation.4 | async-start | bytes 16777216 | tf_op jit(solution)/shard_map/all_to_all | solution.py:147
  429.7 97.4 %all-to-all-start.7 = ((bf16[16,16,4,16,128]{4,3,2,1,0:T(8,128)(2,1)}), bf16[16,16,4,16,128]{4,3,2,1,0:T(8,128)(2,1)}, u32[]{:S(2)}, u32[]{:S(2)}) async-start(bf16[16,16,4,16,128]{4,3,2,1,0:T(8,128)(2,1)} %bitcast.195), calls=%async_computation.7 | async-start | bytes 8388608 | tf_op jit(solution)/shard_map/all_to_all | solution.py:108
  437.1 35.9 %collective-permute-start = (bf16[1,3,1024,256]{2,3,1,0:T(8,128)(2,1)}, bf16[1,3,1024,256]{2,3,1,0:T(8,128)(2,1)}, u32[]{:S(2)}, u32[]{:S(2)}) collective-permute-start(bf16[1,3,1024,256]{2,3,1,0:T(8,128)(2,1)} %copy.122), channel_id=1, source_target_pairs={{0,1},{1,0},{2,3},{3,2},{4,5},{5,4},{6,7},{7,6},{8,9},{9,8},{10,11... | collective-permute-start | bytes 4718600 | tf_op jit(solution)/shard_map/ppermute | solution.py:141
  476.7 1.7 copy-start.4
  504.0 28.3 %copy-start.7 = (f32[256,8]{0,1:T(8,128)S(1)}, f32[256,8]{0,1:T(8,128)}, u32[]{:S(2)}) copy-start(f32[256,8]{0,1:T(8,128)} %param.23) | copy-start | bytes 24580
  527.0 187.5 %all-to-all-start.5 = ((bf16[16,256,1024]{1,2,0:T(8,128)(2,1)}), bf16[16,256,1024]{1,2,0:T(8,128)(2,1)}, u32[]{:S(2)}, u32[]{:S(2)}) async-start(bf16[16,256,1024]{1,2,0:T(8,128)(2,1)} %convert_bitcast_fusion), calls=%async_computation.5 | async-start | bytes 16777216 | tf_op jit(solution)/shard_map/all_to_all | solution.py:160
